TPU v7x, 32 devices: a whole 2x2x4 slice. The times are simulated.
32 devices in a mesh: tile: 8 (over y, x, core), mem: 4 (over z).
Axes of the slice: x: 2, y: 2, z: 4, core: 2. Of those that a mesh axis runs over, the one named last changes fastest.
Arguments:
- control: bfloat16 [80, 1, 360, 720], P('mem', None, 'tile'), may hold values from -6 to 6
- perturb: bfloat16 [80, 1, 360, 720], P('mem', None, 'tile'), may hold values from -6 to 6
- lon_taps: bfloat16 [17], replicated, may hold values from 0.026367188 to 0.07910156
- lat_taps: bfloat16 [17], replicated, may hold values from 0.026367188 to 0.07910156
- innov: float32 [8, 8, 256], P('tile'), may hold values from -6 to 6
- inv_var: float32 [8, 8, 256], P('tile'), may hold values from 1 to 8
- cell_index: int32 [8, 8, 256], P('tile'), may hold values from 0 to 32399, as said below
- counts: int32 [8, 8], P('tile'), may hold values from 0 to 256, as said below
Outputs:
- gradient: float32 [80, 1, 360, 720], P('mem', None, 'tile')
Inputs may be any that keep to these rules, and one draw needn't show every extreme that they name: `cell_index`: an observation's cell within its owning tile, level * 45 * 720 + longitude within the tile * 720 + latitude; both ends are taken. `counts`: live slots per pair of tiles; some pair fills all 256 slots in every draw, and some owning tiles receive far more than others.
All inputs are finite; a program needn't handle non-finite values.
Results may differ from a plain program's by a relative error of at most 0.00066.
Values may be sent and summed in bfloat16 or wider, within the bound.
No kernel may reach another device: no remote copies, remote signals or barrier semaphores. Data moves between devices by JAX's collectives and lax.ppermute only.
A program may use at most 64 MiB of HBM per device.

v0:
```python
import math
import jax
import jax.numpy as jnp
from jax import lax
from jax.sharding import PartitionSpec as P


def extended_2(block, sides, width):
    for axis, dim in sides:
        count = lax.axis_size(axis)
        forward = [(i, i + 1) for i in range(count - 1)]
        forward.append((count - 1, 0))
        backward = [(target, source) for source, target in forward]
        low = lax.ppermute(
            lax.slice_in_dim(block, block.shape[dim] - width, None, axis=dim), axis, forward
        )
        high = lax.ppermute(lax.slice_in_dim(block, 0, width, axis=dim), axis, backward)
        block = jnp.concatenate([low, block, high], axis=dim)
    return block


def band_from(offsets, tap_weights):
    radius = tap_weights.shape[0] - 1
    taps = tap_weights.astype(jnp.float32)
    band = jnp.zeros(offsets.shape, jnp.float32)
    for offset in range(radius + 1):
        band = band + jnp.where(offsets == offset, taps[offset], 0.0)
    return band.astype(jnp.bfloat16)


def lon_band(tap_weights, lon_cells):
    radius = tap_weights.shape[0] - 1
    row_ids = lax.broadcasted_iota(jnp.int32, (lon_cells, lon_cells + 2 * radius), 0)
    col_ids = lax.broadcasted_iota(jnp.int32, (lon_cells, lon_cells + 2 * radius), 1)
    return band_from(jnp.abs(col_ids - row_ids - radius), tap_weights)


def lat_block_band(tap_weights, block_cells):
    radius = tap_weights.shape[0] - 1
    row_ids = lax.broadcasted_iota(jnp.int32, (block_cells + 2 * radius, block_cells), 0)
    col_ids = lax.broadcasted_iota(jnp.int32, (block_cells + 2 * radius, block_cells), 1)
    return band_from(jnp.abs(row_ids - radius - col_ids), tap_weights)


def localize(extended, band_lon, band_blocks, radius, block_cells):
    along = jnp.einsum(
        "ij,mljk->mlik", band_lon, extended, preferred_element_type=jnp.float32
    ).astype(jnp.bfloat16)
    members_here, levels, lon_cells, lat_cells = along.shape
    padded = jnp.pad(along, ((0, 0), (0, 0), (0, 0), (radius, radius)))
    block_count = lat_cells // block_cells
    windows = jnp.stack(
        [
            padded[:, :, :, block * block_cells : block * block_cells + block_cells + 2 * radius]
            for block in range(block_count)
        ],
        axis=3,
    )
    result = jnp.einsum("mlibk,kq->mlibq", windows, band_blocks, preferred_element_type=jnp.float32)
    return result.reshape(members_here, levels, lon_cells, lat_cells)


def pick_cells(field_rows, row_index, col_index, block_rows):
    row_count, col_count = field_rows.shape
    field_cols = field_rows.T

    def pick_one_block(indices):
        rows_here, cols_here = indices
        onehot_rows = (
            rows_here[:, None] == jnp.arange(row_count, dtype=jnp.int32)[None, :]
        ).astype(jnp.float32)
        onehot_cols = (
            cols_here[:, None] == jnp.arange(col_count, dtype=jnp.int32)[None, :]
        ).astype(jnp.float32)
        picked = jnp.dot(
            onehot_cols,
            field_cols,
            precision=lax.Precision.HIGHEST,
            preferred_element_type=jnp.float32,
        )
        return jnp.sum(picked * onehot_rows, axis=1)

    values = lax.map(
        pick_one_block, (row_index.reshape(-1, block_rows), col_index.reshape(-1, block_rows))
    )
    return values.reshape(-1)


def spread_cells(misfit, row_index, col_index, row_count, col_count, block_rows):

    def spread_one_block(total, items):
        rows_here, cols_here, values = items
        onehot_rows = (
            rows_here[:, None] == jnp.arange(row_count, dtype=jnp.int32)[None, :]
        ).astype(jnp.float32)
        onehot_cols = (
            cols_here[:, None] == jnp.arange(col_count, dtype=jnp.int32)[None, :]
        ).astype(jnp.float32)
        weighted = onehot_rows * values[:, None]
        return (
            total
            + jnp.dot(
                weighted.T,
                onehot_cols,
                precision=lax.Precision.HIGHEST,
                preferred_element_type=jnp.float32,
            ),
            None,
        )

    start = jnp.zeros((row_count, col_count), jnp.float32)
    items = (
        row_index.reshape(-1, block_rows),
        col_index.reshape(-1, block_rows),
        misfit.reshape(-1, block_rows),
    )
    total, _ = lax.scan(spread_one_block, start, items)
    return total


def local(control, perturb, lon_taps, lat_taps, innov, inv_var, cell_index, counts):
    members_here, levels, lon_cells, lat_cells = control.shape
    radius = lon_taps.shape[0] - 1
    block_cells = 144
    band_lon = lon_band(lon_taps, lon_cells)
    band_blocks = lat_block_band(lat_taps, block_cells)
    extended = extended_2(control, (("tile", 2),), radius)
    smoothed = localize(extended, band_lon, band_blocks, radius, block_cells)
    member_sum = jnp.sum(perturb.astype(jnp.float32) * smoothed, axis=0)
    slot_ids = lax.broadcasted_iota(jnp.int32, innov.shape, 2)
    is_live = slot_ids < counts[:, :, None]
    weights = jnp.where(is_live, inv_var, 0.0)
    received = (
        lax.all_to_all(innov, "tile", split_axis=1, concat_axis=0, tiled=True),
        lax.all_to_all(weights, "tile", split_axis=1, concat_axis=0, tiled=True),
        lax.all_to_all(cell_index, "tile", split_axis=1, concat_axis=0, tiled=True),
    )
    observed = received[0].reshape(-1)
    weight_recv = received[1].reshape(-1)
    cells_hit = received[2].reshape(-1)
    row_index = cells_hit // lat_cells
    col_index = cells_hit % lat_cells
    row_count = levels * lon_cells
    block_rows = math.gcd(observed.shape[0], 1024)
    increment = lax.psum(member_sum, "mem")
    at_cells = pick_cells(increment.reshape(row_count, lat_cells), row_index, col_index, block_rows)
    misfit = weight_recv * (at_cells - observed)
    spread = spread_cells(misfit, row_index, col_index, row_count, lat_cells, block_rows)
    spread = spread.reshape(levels, lon_cells, lat_cells)
    wide_pert = extended_2(perturb, (("tile", 2),), radius)
    wide_spread = extended_2(spread, (("tile", 1),), radius)
    wide_products = (wide_pert.astype(jnp.float32) * wide_spread[None]).astype(jnp.bfloat16)
    return control.astype(jnp.float32) + localize(
        wide_products, band_lon, band_blocks, radius, block_cells
    )


def solution(mesh):
    return jax.shard_map(
        local,
        mesh=mesh,
        in_specs=(
            P("mem", None, "tile", None),
            P("mem", None, "tile", None),
            P(),
            P(),
            P("tile", None, None),
            P("tile", None, None),
            P("tile", None, None),
            P("tile", None),
        ),
        out_specs=P("mem", None, "tile", None),
        check_vma=False,
    )
```

profile of v0, /device:TPU:11, one launch (start us, length us, event | category | flops | bytes accessed | tf_op | source)
XLA Modules:
  0.0 176.9 jit_solution(8008073635435257452)
XLA Ops:
  8.1 1.8 %collective-permute-start.2 = (bf16[20,1,16,720]{3,2,0,1:T(8,128)(2,1)S(1)}, bf16[20,1,16,720]{3,2,0,1:T(8,128)(2,1)}, u32[]{:S(2)}, u32[]{:S(2)}) collective-permute-start(bf16[20,1,16,720]{3,2,0,1:T(8,128)(2,1)S(1)} %get-tuple-element.115), channel_id=1, source_target_pairs={{0,4},{4,8},{8,12},{12,16},{16,20},{20,24},{24,28},{28,0},{1,5},{5... | collective-permute-start | bytes 1382408 | tf_op jit(solution)/shard_map/ppermute | solution.py:14
  11.2 4.9 %all-to-all-start = ((s32[1,8,256]{2,0,1:T(1,128)}), s32[1,8,256]{2,0,1:T(1,128)S(1)}, u32[]{:S(2)}, u32[]{:S(2)}) async-start(s32[1,8,256]{2,0,1:T(1,128)} %copy.48), calls=%async_computation | async-start | bytes 16384 | tf_op jit(solution)/shard_map/all_to_all | solution.py:136
  16.1 2.2 %fusion.167 = (bf16[20,1,16,720]{3,2,0,1:T(8,128)(2,1)}, bf16[20,1,16,720]{3,2,0,1:T(8,128)(2,1)S(1)}) fusion(bf16[20,1,45,720]{3,2,0,1:T(8,128)(2,1)} %bitcast.147), kind=kLoop, calls=%fused_computation.200 | loop fusion | bytes 1843200 | tf_op jit(solution)/shard_map/slice | solution.py:15
  23.2 4.4 %all-to-all-start.1 = ((f32[1,8,256]{2,0,1:T(1,128)}), f32[1,8,256]{2,0,1:T(1,128)S(1)}, u32[]{:S(2)}, u32[]{:S(2)}) async-start(f32[1,8,256]{2,0,1:T(1,128)} %compare_select_fusion), calls=%async_computation.1 | async-start | bytes 16384 | tf_op jit(solution)/shard_map/all_to_all | solution.py:135
  27.7 5.6 %all-to-all-done.1 = f32[1,8,256]{2,0,1:T(1,128)S(1)} async-done(((f32[1,8,256]{2,0,1:T(1,128)}), f32[1,8,256]{2,0,1:T(1,128)S(1)}, u32[]{:S(2)}, u32[]{:S(2)}) %all-to-all-start.1) | async-done | bytes 8224 | tf_op jit(solution)/shard_map/all_to_all | solution.py:135
  33.4 4.0 %all-to-all-start.2 = ((f32[1,8,256]{2,0,1:T(1,128)}), f32[1,8,256]{2,0,1:T(1,128)S(1)}, u32[]{:S(2)}, u32[]{:S(2)}) async-start(f32[1,8,256]{2,0,1:T(1,128)} %copy.57), calls=%async_computation.2 | async-start | bytes 16384 | tf_op jit(solution)/shard_map/all_to_all | solution.py:134
  37.5 3.1 %all-to-all-done.2 = f32[1,8,256]{2,0,1:T(1,128)S(1)} async-done(((f32[1,8,256]{2,0,1:T(1,128)}), f32[1,8,256]{2,0,1:T(1,128)S(1)}, u32[]{:S(2)}, u32[]{:S(2)}) %all-to-all-start.2) | async-done | bytes 8224 | tf_op jit(solution)/shard_map/all_to_all | solution.py:134
  40.7 12.1 %fusion.31 = bf16[20,1,45,720]{3,2,0,1:T(8,128)(2,1)S(1)} fusion(bf16[20,1,16,720]{3,2,0,1:T(8,128)(2,1)} %collective-permute-done.3, bf16[20,1,45,720]{3,2,0,1:T(8,128)(2,1)S(1)} %bitcast.146, bf16[20,1,16,720]{3,2,0,1:T(8,128)(2,1)} %collective-permute-done.2, f32[]{:T(128)} %bitcast.31, f32[]{:T(128)} %bitcast.30, f32[]{:T(128)} %bitcast.29, ...), kind=kOutput, calls=%fused_computation.44 | convolution fusion | flops 107279912 | bytes 3513668 | tf_op jit(solution)/shard_map/ij,mljk->mlik/dot_general | solution.py:46
  53.7 11.5 %fusion.25 = f32[20,45,5,144]{3,1,2,0:T(8,128)S(1)} fusion(f32[]{:T(128)} %bitcast.58, f32[]{:T(128)} %bitcast.57, f32[]{:T(128)} %bitcast.56, f32[]{:T(128)} %bitcast.55, f32[]{:T(128)} %bitcast.54, f32[]{:T(128)} %bitcast.53, f32[]{:T(128)} %bitcast.52, f32[]{:T(128)} %bitcast.51, f32[]{:T(128)} %bitcast.50, f32[]{:T(128)} %bitcast.49, f32[]{:T(128)} %bitcast.48, ...), kind=kOutput, calls=%fused_computation.38 | convolution fusion | flops 229439232 | bytes 4176772 | tf_op jit(solution)/shard_map/mlibk,kq->mlibq/dot_general | solution.py:59
  65.2 6.4 %copy.55 = f32[20,45,5,144]{3,2,1,0:T(8,128)} copy(f32[20,45,5,144]{3,1,2,0:T(8,128)S(1)} %fusion.25) | data formatting | bytes 5184000 | tf_op jit(solution)/shard_map/mlibk,kq->mlibq/dot_general | solution.py:59
  71.6 4.9 %reshape.136 = f32[20,1,45,720]{3,2,0,1:T(8,128)S(1)} reshape(f32[20,45,5,144]{3,2,1,0:T(8,128)} %copy.55) | data formatting | bytes 5184000 | tf_op jit(solution)/shard_map/reshape | solution.py:60
  76.4 2.4 %multiply_reduce_fusion = f32[45,720]{1,0:T(8,128)} fusion(f32[20,1,45,720]{3,2,0,1:T(8,128)S(1)} %reshape.136, bf16[20,1,45,720]{3,2,1,0:T(8,128)(2,1)} %param.13), kind=kLoop, calls=%fused_computation.22 | loop fusion | flops 1911600 | bytes 4017600 | tf_op jit(solution)/shard_map/reduce_sum | solution.py:129
  78.9 32.7 %all-reduce.4.cloned.1.call-done = f32[720,45]{0,1:T(8,128)} async-done(((f32[720,45]{0,1:T(8,128)}), f32[720,45]{0,1:T(8,128)}) %all-reduce.4.cloned.1.call-update) | async-done | bytes 129616 | tf_op jit(solution)/shard_map/psum | solution.py:145
  112.7 3.8 %while.21 = (s32[]{:T(128)}, f32[2,1024]{1,0:T(2,128)S(1)}, s32[2,1024]{1,0:T(2,128)S(1)}, s32[2,1024]{1,0:T(2,128)S(1)}, f32[720,45]{1,0:T(8,128)S(1)}, /*index=5*/s32[]{:T(128)}, s32[]{:T(128)}) while((s32[]{:T(128)}, f32[2,1024]{1,0:T(2,128)S(1)}, s32[2,1024]{1,0:T(2,128)S(1)}, s32[2,1024]{1,0:T(2,128)S(1)}, f32[720,45]{1,0:T(8,128)S(1)}, ...), condition=%wide.region_4.5_spmd, body=%wide.region_2.4_spmd.sunk | while | flops 399005696 | bytes 166549 | solution.py:83
  112.7 1.8 %fusion.179 = f32[1024]{0:T(1024)S(1)} fusion(f32[720,45]{1,0:T(8,128)S(1)} %get-tuple-element.245, s32[1024]{0:T(1024)S(1)} %bitcast.156, s32[1024]{0:T(1024)S(1)} %bitcast.157), kind=kOutput, calls=%fused_computation.4.clone.1 | convolution fusion | flops 399005696 | bytes 141888 | tf_op jit(solution)/shard_map/while/body/eval_jaxpr/dot_general | solution.py:75
  114.6 1.8 %fusion.179 = f32[1024]{0:T(1024)S(1)} fusion(f32[720,45]{1,0:T(8,128)S(1)} %get-tuple-element.245, s32[1024]{0:T(1024)S(1)} %bitcast.156, s32[1024]{0:T(1024)S(1)} %bitcast.157), kind=kOutput, calls=%fused_computation.4.clone.1 | convolution fusion | flops 399005696 | bytes 141888 | tf_op jit(solution)/shard_map/while/body/eval_jaxpr/dot_general | solution.py:75
  116.5 3.1 %while.22 = (s32[]{:T(128)}, f32[45,720]{1,0:T(8,128)S(1)}, s32[2,1024]{1,0:T(2,128)S(1)}, f32[2,1024]{1,0:T(2,128)S(1)}, s32[2,1024]{1,0:T(2,128)S(1)}, /*index=5*/s32[]{:T(128)}, s32[]{:T(128)}) while((s32[]{:T(128)}, f32[45,720]{1,0:T(8,128)S(1)}, s32[2,1024]{1,0:T(2,128)S(1)}, f32[2,1024]{1,0:T(2,128)S(1)}, ...), condition=%wide.region_6.7_spmd.clone, body=%wide.region_5.6_spmd.clone.sunk | while | flops 399025440 | bytes 296159 | solution.py:117
  119.7 3.9 %collective-permute-start.4 = (f32[1,16,720]{2,1,0:T(8,128)S(1)}, f32[1,16,720]{2,1,0:T(8,128)S(1)}, u32[]{:S(2)}, u32[]{:S(2)}) collective-permute-start(f32[1,16,720]{2,1,0:T(8,128)S(1)} %get-tuple-element.119), channel_id=1, source_target_pairs={{0,4},{4,8},{8,12},{12,16},{16,20},{20,24},{24,28},{28,0},{1,5},{5... | collective-permute-start | bytes 138248 | tf_op jit(solution)/shard_map/ppermute | solution.py:14
  124.7 3.2 %collective-permute-done.5 = f32[1,16,720]{2,1,0:T(8,128)S(1)} collective-permute-done((f32[1,16,720]{2,1,0:T(8,128)S(1)}, f32[1,16,720]{2,1,0:T(8,128)S(1)}, u32[]{:S(2)}, u32[]{:S(2)}) %collective-permute-start.5) | collective-permute-done | bytes 46112 | tf_op jit(solution)/shard_map/ppermute | solution.py:17
  128.0 12.3 %fusion.30 = bf16[20,1,45,720]{3,2,0,1:T(8,128)(2,1)S(1)} fusion(bf16[20,16,720]{2,1,0:T(8,128)(2,1)} %bitcast.8, bf16[20,45,720]{2,1,0:T(8,128)(2,1)S(1)} %bitcast.148, bf16[20,16,720]{2,1,0:T(8,128)(2,1)} %bitcast.5, f32[77,720]{1,0:T(8,128)S(1)} %maximum_bitcast_fusion.6, f32[]{:T(128)} %bitcast.31, f32[]{:T(128)} %bitcast.30, f32[]{:T(128)} %bitcast.29, ...), kind=kOutput, calls=%fused_computation.43 | convolution fusion | flops 109497512 | bytes 3735428 | tf_op jit(solution)/shard_map/ij,mljk->mlik/dot_general | solution.py:46
  141.2 11.5 %fusion.23 = f32[20,45,5,144]{3,1,2,0:T(8,128)S(1)} fusion(f32[]{:T(128)} %bitcast.58, f32[]{:T(128)} %bitcast.57, f32[]{:T(128)} %bitcast.56, f32[]{:T(128)} %bitcast.55, f32[]{:T(128)} %bitcast.54, f32[]{:T(128)} %bitcast.53, f32[]{:T(128)} %bitcast.52, f32[]{:T(128)} %bitcast.51, f32[]{:T(128)} %bitcast.50, f32[]{:T(128)} %bitcast.49, f32[]{:T(128)} %bitcast.48, ...), kind=kOutput, calls=%fused_computation.36 | convolution fusion | flops 229439232 | bytes 4176772 | tf_op jit(solution)/shard_map/mlibk,kq->mlibq/dot_general | solution.py:59
  152.7 6.4 %copy.59 = f32[20,45,5,144]{3,2,1,0:T(8,128)} copy(f32[20,45,5,144]{3,1,2,0:T(8,128)S(1)} %fusion.23) | data formatting | bytes 5184000 | tf_op jit(solution)/shard_map/mlibk,kq->mlibq/dot_general | solution.py:59
  159.1 4.9 %reshape.141 = f32[20,1,45,720]{3,2,0,1:T(8,128)S(1)} reshape(f32[20,45,5,144]{3,2,1,0:T(8,128)} %copy.59) | data formatting | bytes 5184000 | tf_op jit(solution)/shard_map/reshape | solution.py:60
  165.7 4.4 %copy.60 = f32[20,1,45,720]{3,1,2,0:T(1,128)} copy(f32[20,1,45,720]{3,2,0,1:T(8,128)S(1)} %convert_add_fusion) | data formatting | bytes 5184000 | tf_op jit(solution)/shard_map/add | solution.py:153
  (72 shorter events, 16.9 us)
Async XLA Ops:
  6.5 34.1 %copy-start = (bf16[20,1,45,720]{3,2,1,0:T(8,128)(2,1)S(1)}, bf16[20,1,45,720]{3,2,1,0:T(8,128)(2,1)}, u32[]{:S(2)}) copy-start(bf16[20,1,45,720]{3,2,1,0:T(8,128)(2,1)} %param.12) | copy-start | bytes 3888004
  6.5 13.2 %copy-start.7 = (s32[1,8]{1,0:T(1,128)S(1)}, s32[1,8]{1,0:T(1,128)}, u32[]{:S(2)}) copy-start(s32[1,8]{1,0:T(1,128)} %param.19) | copy-start | bytes 100
  6.5 13.2 %copy-start.5 = (f32[1,8,256]{2,1,0:T(8,128)S(1)}, f32[1,8,256]{2,1,0:T(8,128)}, u32[]{:S(2)}) copy-start(f32[1,8,256]{2,1,0:T(8,128)} %param.17) | copy-start | bytes 24580
  6.5 13.9 %copy-start.3 = (bf16[17]{0:T(256)(128)(2,1)S(1)}, bf16[17]{0:T(256)(128)(2,1)}, u32[]{:S(2)}) copy-start(bf16[17]{0:T(256)(128)(2,1)} %param.14) | copy-start | bytes 106
  6.5 14.6 %copy-start.4 = (bf16[17]{0:T(256)(128)(2,1)S(1)}, bf16[17]{0:T(256)(128)(2,1)}, u32[]{:S(2)}) copy-start(bf16[17]{0:T(256)(128)(2,1)} %param.15) | copy-start | bytes 106
  6.5 15.3 %copy-start.6 = (f32[1,8,256]{2,1,0:T(8,128)S(1)}, f32[1,8,256]{2,1,0:T(8,128)}, u32[]{:S(2)}) copy-start(f32[1,8,256]{2,1,0:T(8,128)} %param.16) | copy-start | bytes 24580
  8.1 32.6 %collective-permute-start.2 = (bf16[20,1,16,720]{3,2,0,1:T(8,128)(2,1)S(1)}, bf16[20,1,16,720]{3,2,0,1:T(8,128)(2,1)}, u32[]{:S(2)}, u32[]{:S(2)}) collective-permute-start(bf16[20,1,16,720]{3,2,0,1:T(8,128)(2,1)S(1)} %get-tuple-element.115), channel_id=1, source_target_pairs={{0,4},{4,8},{8,12},{12,16},{16,20},{20,24},{24,28},{28,0},{1,5},{5... | collective-permute-start | bytes 1382408 | tf_op jit(solution)/shard_map/ppermute | solution.py:14
  9.9 30.7 %collective-permute-start.3 = (bf16[20,1,16,720]{3,2,0,1:T(8,128)(2,1)S(1)}, bf16[20,1,16,720]{3,2,0,1:T(8,128)(2,1)}, u32[]{:S(2)}, u32[]{:S(2)}) collective-permute-start(bf16[20,1,16,720]{3,2,0,1:T(8,128)(2,1)S(1)} %get-tuple-element.116), channel_id=1, source_target_pairs={{4,0},{8,4},{12,8},{16,12},{20,16},{24,20},{28,24},{0,28},{5,1},{9... | collective-permute-start | bytes 1382408 | tf_op jit(solution)/shard_map/ppermute | solution.py:17
  11.2 12.0 %all-to-all-start = ((s32[1,8,256]{2,0,1:T(1,128)}), s32[1,8,256]{2,0,1:T(1,128)S(1)}, u32[]{:S(2)}, u32[]{:S(2)}) async-start(s32[1,8,256]{2,0,1:T(1,128)} %copy.48), calls=%async_computation | async-start | bytes 16384 | tf_op jit(solution)/shard_map/all_to_all | solution.py:136
  18.3 109.7 %collective-permute-start = (bf16[20,1,16,720]{3,2,0,1:T(8,128)(2,1)}, bf16[20,1,16,720]{3,2,0,1:T(8,128)(2,1)}, u32[]{:S(2)}, u32[]{:S(2)}) collective-permute-start(bf16[20,1,16,720]{3,2,0,1:T(8,128)(2,1)} %get-tuple-element.117), channel_id=1, source_target_pairs={{0,4},{4,8},{8,12},{12,16},{16,20},{20,24},{24,28},{28,0},{1,5},{5... | collective-permute-start | bytes 1382408 | tf_op jit(solution)/shard_map/ppermute | solution.py:14
  19.8 108.2 %collective-permute-start.1 = (bf16[20,1,16,720]{3,2,0,1:T(8,128)(2,1)S(1)}, bf16[20,1,16,720]{3,2,0,1:T(8,128)(2,1)}, u32[]{:S(2)}, u32[]{:S(2)}) collective-permute-start(bf16[20,1,16,720]{3,2,0,1:T(8,128)(2,1)S(1)} %get-tuple-element.118), channel_id=1, source_target_pairs={{4,0},{8,4},{12,8},{16,12},{20,16},{24,20},{28,24},{0,28},{5,1},{9... | collective-permute-start | bytes 1382408 | tf_op jit(solution)/shard_map/ppermute | solution.py:17
  23.2 10.1 %all-to-all-start.1 = ((f32[1,8,256]{2,0,1:T(1,128)}), f32[1,8,256]{2,0,1:T(1,128)S(1)}, u32[]{:S(2)}, u32[]{:S(2)}) async-start(f32[1,8,256]{2,0,1:T(1,128)} %compare_select_fusion), calls=%async_computation.1 | async-start | bytes 16384 | tf_op jit(solution)/shard_map/all_to_all | solution.py:135
  33.4 7.2 %all-to-all-start.2 = ((f32[1,8,256]{2,0,1:T(1,128)}), f32[1,8,256]{2,0,1:T(1,128)S(1)}, u32[]{:S(2)}, u32[]{:S(2)}) async-start(f32[1,8,256]{2,0,1:T(1,128)} %copy.57), calls=%async_computation.2 | async-start | bytes 16384 | tf_op jit(solution)/shard_map/all_to_all | solution.py:134
  37.3 74.3 %all-reduce.4.cloned.1.call-start = ((), (), s32[]{:S(2)}) async-start(), calls=%async_computation.3 | async-start | bytes 294912 | tf_op jit(solution)/shard_map/psum | solution.py:145
  112.7 3.8 %copy-start.2 = (f32[45,720]{1,0:T(8,128)S(1)}, f32[45,720]{1,0:T(8,128)}, u32[]{:S(2)}) copy-start(f32[45,720]{1,0:T(8,128)} %custom-call) | copy-start | bytes 388804
  116.5 11.5 %copy-start.1 = (bf16[20,1,45,720]{3,2,1,0:T(8,128)(2,1)S(1)}, bf16[20,1,45,720]{3,2,1,0:T(8,128)(2,1)}, u32[]{:S(2)}) copy-start(bf16[20,1,45,720]{3,2,1,0:T(8,128)(2,1)} %param.13) | copy-start | bytes 3888004
  119.7 5.1 %collective-permute-start.4 = (f32[1,16,720]{2,1,0:T(8,128)S(1)}, f32[1,16,720]{2,1,0:T(8,128)S(1)}, u32[]{:S(2)}, u32[]{:S(2)}) collective-permute-start(f32[1,16,720]{2,1,0:T(8,128)S(1)} %get-tuple-element.119), channel_id=1, source_target_pairs={{0,4},{4,8},{8,12},{12,16},{16,20},{20,24},{24,28},{28,0},{1,5},{5... | collective-permute-start | bytes 138248 | tf_op jit(solution)/shard_map/ppermute | solution.py:14
  123.5 4.4 %collective-permute-start.5 = (f32[1,16,720]{2,1,0:T(8,128)S(1)}, f32[1,16,720]{2,1,0:T(8,128)S(1)}, u32[]{:S(2)}, u32[]{:S(2)}) collective-permute-start(f32[1,16,720]{2,1,0:T(8,128)S(1)} %get-tuple-element.120), channel_id=1, source_target_pairs={{4,0},{8,4},{12,8},{16,12},{20,16},{24,20},{28,24},{0,28},{5,1},{9... | collective-permute-start | bytes 138248 | tf_op jit(solution)/shard_map/ppermute | solution.py:17
Sparse Core Ops, SparseCore 0:
  79.0 32.5 all-reduce.3
where the time goes:
time: 178 us; the launch traced here: 177 us
  matrix products  54 us (30%)
  waiting for transfers between devices  46.7 us (26%)
  local copies, waits for them, and re-layouts  37 us (21%)
  starting transfers between devices  20.5 us (12%)
  between operations  13.7 us (8%)
  other arithmetic  4.93 us (3%)
    psum x1, waiting for transfers between devices, local(): increment = lax.psum(member_sum, 'mem')  32.7 us
    dot_general x2, matrix products, localize(): jnp.einsum('ij,mljk->mlik', band_lon, extended, preferred_element_type=jn...  24.4 us
    dot_general x2, matrix products, localize(): jnp.einsum('mlibk,kq->mlibq', windows, band_blocks, preferred_element_typ...  23 us
    dot_general x2, local copies, waits for them, and re-layouts, localize(): jnp.einsum('mlibk,kq->mlibq', windows, band_blocks, preferred_element_typ...  12.8 us
    reshape x2, local copies, waits for them, and re-layouts, localize(): return result.reshape(members_here, levels, lon_cells, lat_cells)  9.75 us
    ppermute x3, starting transfers between devices, extended_2(): lax.ppermute(lax.slice_in_dim(block, block.shape[dim] - width, None, axis...  7.17 us
    all_to_all x1, waiting for transfers between devices, local(): lax.all_to_all(weights, 'tile', split_axis=1, concat_axis=0, tiled=True)  5.65 us
    all_to_all x1, starting transfers between devices, local(): lax.all_to_all(cell_index, 'tile', split_axis=1, concat_axis=0, tiled=True)  4.92 us
  transfers between devices with their start and end apart: 10, of which 6 were waited for; matrix products, arithmetic and copies ran while one was open for 30% of the time, Pallas kernels for 0%

commit v1 on v0

--- a/solution.py
+++ b/solution.py
@@ -3,6 +3,35 @@
 import jax.numpy as jnp
 from jax import lax
 from jax.sharding import PartitionSpec as P
+
+
+def cut_flows(shard_in, d0, inner_x):
+    block_last = shard_in.shape
+    w2 = shard_in.reshape(
+        *block_last[:d0], inner_x, block_last[d0] // inner_x, *block_last[d0 + 1 :]
+    )
+    return jnp.moveaxis(w2, d0, 0)
+
+
+def group_the_panel(vector, pos_dim):
+    vector = jnp.moveaxis(vector, 0, pos_dim)
+    m_next = vector.shape
+    return vector.reshape(
+        *m_next[:pos_dim], m_next[pos_dim] * m_next[pos_dim + 1], *m_next[pos_dim + 2 :]
+    )
+
+
+def map_streams_now(patch, mesh_ax, field_in, m):
+    long_array, plain = (jax.lax.axis_size(mesh_ax), jax.lax.axis_index(mesh_ax))
+    part_next = cut_flows(patch, field_in, long_array)
+    leaves = [part_next[plain]]
+    for p in tuple(range(1, long_array)):
+        o_now = part_next[plain ^ p]
+        leaves.append(
+            jax.lax.ppermute(o_now, axis_name=mesh_ax, perm=[(h, h ^ p) for h in range(long_array)])
+        )
+    part_next = jnp.stack(leaves, axis=0)[plain ^ jnp.arange(long_array)]
+    return group_the_panel(part_next, m)
 
 
 def extended_2(block, sides, width):
@@ -133,7 +162,7 @@
     received = (
         lax.all_to_all(innov, "tile", split_axis=1, concat_axis=0, tiled=True),
         lax.all_to_all(weights, "tile", split_axis=1, concat_axis=0, tiled=True),
-        lax.all_to_all(cell_index, "tile", split_axis=1, concat_axis=0, tiled=True),
+        map_streams_now(cell_index, "tile", 1, 0),
     )
     observed = received[0].reshape(-1)
     weight_recv = received[1].reshape(-1)

time: 178 us -> 174 us (0.978)
  waiting for transfers between devices: 46.7 us -> 36.6 us
  local copies, waits for them, and re-layouts: 37 us -> 39.8 us
  starting transfers between devices: 20.5 us -> 22.7 us
    psum x1, waiting for transfers between devices: 32.7 us -> 26 us  [local(): increment = lax.psum(member_sum, 'mem')]
    ppermute x0 -> x7, starting transfers between devices: none -> 6.23 us  [map_streams_now(): jax.lax.ppermute(o_now, axis_name=mesh_ax, perm=[(h, h ^ p) for h in rang...]
    all_to_all x1, waiting for transfers between devices: 5.65 us -> 0.01 us  [local(): lax.all_to_all(weights, 'tile', split_axis=1, concat_axis=0, tiled=True)]
    all_to_all x1 -> x0, starting transfers between devices: 4.92 us -> none  [local(): lax.all_to_all(cell_index, 'tile', split_axis=1, concat_axis=0, tiled=True)]
    ppermute x0 -> x7, waiting for transfers between devices: none -> 2.92 us  [map_streams_now(): jax.lax.ppermute(o_now, axis_name=mesh_ax, perm=[(h, h ^ p) for h in rang...]
    slice x2, local copies, waits for them, and re-layouts: 1.41 us -> 3.97 us  [band_from(): band = band + jnp.where(offsets == offset, taps[offset], 0.0)]
  transfers between devices with their start and end apart: 10 -> 16, of which waited for: 6 -> 5; matrix products, arithmetic and copies ran while one was open for 30% -> 32% of each run, Pallas kernels for 0% -> 0%
where the time goes in v1:
time: 174 us; the launch traced here: 173 us
  matrix products  54.3 us (31%)
  local copies, waits for them, and re-layouts  39.8 us (23%)
  waiting for transfers between devices  36.6 us (21%)
  starting transfers between devices  22.7 us (13%)
  between operations  13.7 us (8%)
  other arithmetic  5.55 us (3%)
    psum x1, waiting for transfers between devices, local(): increment = lax.psum(member_sum, 'mem')  26 us
    dot_general x2, matrix products, localize(): jnp.einsum('ij,mljk->mlik', band_lon, extended, preferred_element_type=jn...  25.2 us
    dot_general x2, matrix products, localize(): jnp.einsum('mlibk,kq->mlibq', windows, band_blocks, preferred_element_typ...  22.6 us
    dot_general x2, local copies, waits for them, and re-layouts, localize(): jnp.einsum('mlibk,kq->mlibq', windows, band_blocks, preferred_element_typ...  12.8 us
    reshape x2, local copies, waits for them, and re-layouts, localize(): return result.reshape(members_here, levels, lon_cells, lat_cells)  9.75 us
    ppermute x3, starting transfers between devices, extended_2(): lax.ppermute(lax.slice_in_dim(block, block.shape[dim] - width, None, axis...  6.53 us
    ppermute x7, starting transfers between devices, map_streams_now(): jax.lax.ppermute(o_now, axis_name=mesh_ax, perm=[(h, h ^ p) for h in rang...  6.23 us
    all_to_all x1, starting transfers between devices, local(): lax.all_to_all(innov, 'tile', split_axis=1, concat_axis=0, tiled=True)  4.97 us
  transfers between devices with their start and end apart: 16, of which 5 were waited for; matrix products, arithmetic and copies ran while one was open for 32% of the time, Pallas kernels for 0%

profile of v1, /device:TPU:11, one launch (start us, length us, event | category | flops | bytes accessed | tf_op | source)
XLA Modules:
  0.0 172.8 jit_solution(12992460935596948629)
XLA Ops:
  9.9 2.1 %collective-permute-start.3 = (s32[1,1,256]{2,1,0:T(1,128)S(1)}, s32[1,1,256]{2,1,0:T(1,128)S(1)}, u32[]{:S(2)}, u32[]{:S(2)}) collective-permute-start(s32[1,1,256]{2,1,0:T(1,128)S(1)} %get-tuple-element.127), channel_id=1, source_target_pairs={{0,8},{4,12},{8,0},{12,4},{16,24},{20,28},{24,16},{28,20},{1,9},{5... | collective-permute-start | bytes 3080 | tf_op jit(solution)/shard_map/ppermute | solution.py:31
  14.6 4.2 %all-to-all-start = ((f32[1,8,256]{2,0,1:T(1,128)}), f32[1,8,256]{2,0,1:T(1,128)S(1)}, u32[]{:S(2)}, u32[]{:S(2)}) async-start(f32[1,8,256]{2,0,1:T(1,128)} %compare_select_fusion), calls=%async_computation | async-start | bytes 16384 | tf_op jit(solution)/shard_map/all_to_all | solution.py:164
  18.9 2.0 %fusion.172 = (f32[1]{0:T(128)}, f32[1]{0:T(128)}, f32[1]{0:T(128)}, f32[1]{0:T(128)}, f32[1]{0:T(128)}, /*index=5*/f32[1]{0:T(128)}, f32[1]{0:T(128)}, f32[1]{0...) fusion(bf16[17]{0:T(256)(128)(2,1)} %param.14), kind=kLoop, calls=%fused_computation.216 | loop fusion | bytes 136 | tf_op jit(solution)/shard_map/slice | solution.py:56
  20.9 2.0 %fusion.171 = (f32[1]{0:T(128)}, f32[1]{0:T(128)}, f32[1]{0:T(128)}, f32[1]{0:T(128)}, f32[1]{0:T(128)}, /*index=5*/f32[1]{0:T(128)}, f32[1]{0:T(128)}, f32[1]{0...) fusion(bf16[17]{0:T(256)(128)(2,1)} %param.15), kind=kLoop, calls=%fused_computation.215 | loop fusion | bytes 136 | tf_op jit(solution)/shard_map/slice | solution.py:56
  22.8 2.2 %fusion.169 = (bf16[20,1,16,720]{3,2,0,1:T(8,128)(2,1)}, bf16[20,1,16,720]{3,2,0,1:T(8,128)(2,1)S(1)}) fusion(bf16[20,1,45,720]{3,2,0,1:T(8,128)(2,1)} %bitcast.159), kind=kLoop, calls=%fused_computation.213 | loop fusion | bytes 1843200 | tf_op jit(solution)/shard_map/slice | solution.py:44
  31.1 2.9 %collective-permute-done.7 = s32[1,1,256]{2,1,0:T(1,128)S(1)} collective-permute-done((s32[1,1,256]{2,1,0:T(1,128)S(1)}, s32[1,1,256]{2,1,0:T(1,128)S(1)}, u32[]{:S(2)}, u32[]{:S(2)}) %collective-permute-start.7) | collective-permute-done | bytes 1056 | tf_op jit(solution)/shard_map/ppermute | solution.py:31
  34.7 12.5 %fusion.31 = bf16[20,1,45,720]{3,2,0,1:T(8,128)(2,1)S(1)} fusion(bf16[20,1,16,720]{3,2,0,1:T(8,128)(2,1)} %collective-permute-done.10, bf16[20,1,45,720]{3,2,0,1:T(8,128)(2,1)S(1)} %bitcast.158, bf16[20,1,16,720]{3,2,0,1:T(8,128)(2,1)} %collective-permute-done.9, f32[]{:T(128)} %bitcast.41, f32[]{:T(128)} %bitcast.40, f32[]{:T(128)} %bitcast.39, ...), kind=kOutput, calls=%fused_computation.45 | convolution fusion | flops 107279912 | bytes 3513668 | tf_op jit(solution)/shard_map/ij,mljk->mlik/dot_general | solution.py:75
  48.1 11.3 %fusion.25 = f32[20,45,5,144]{3,1,2,0:T(8,128)S(1)} fusion(f32[]{:T(128)} %bitcast.68, f32[]{:T(128)} %bitcast.67, f32[]{:T(128)} %bitcast.66, f32[]{:T(128)} %bitcast.65, f32[]{:T(128)} %bitcast.64, f32[]{:T(128)} %bitcast.63, f32[]{:T(128)} %bitcast.62, f32[]{:T(128)} %bitcast.61, f32[]{:T(128)} %bitcast.60, f32[]{:T(128)} %bitcast.59, f32[]{:T(128)} %bitcast.58, ...), kind=kOutput, calls=%fused_computation.39 | convolution fusion | flops 229439232 | bytes 4176772 | tf_op jit(solution)/shard_map/mlibk,kq->mlibq/dot_general | solution.py:88
  59.4 6.4 %copy.53 = f32[20,45,5,144]{3,2,1,0:T(8,128)} copy(f32[20,45,5,144]{3,1,2,0:T(8,128)S(1)} %fusion.25) | data formatting | bytes 5184000 | tf_op jit(solution)/shard_map/mlibk,kq->mlibq/dot_general | solution.py:88
  65.8 4.9 %reshape.162 = f32[20,1,45,720]{3,2,0,1:T(8,128)S(1)} reshape(f32[20,45,5,144]{3,2,1,0:T(8,128)} %copy.53) | data formatting | bytes 5184000 | tf_op jit(solution)/shard_map/reshape | solution.py:89
  70.6 2.4 %multiply_reduce_fusion = f32[45,720]{1,0:T(8,128)} fusion(f32[20,1,45,720]{3,2,0,1:T(8,128)S(1)} %reshape.162, bf16[20,1,45,720]{3,2,1,0:T(8,128)(2,1)} %param.13), kind=kLoop, calls=%fused_computation.23 | loop fusion | flops 1911600 | bytes 4017600 | tf_op jit(solution)/shard_map/reduce_sum | solution.py:158
  73.1 5.0 %all-to-all-start.1 = ((f32[1,8,256]{2,0,1:T(1,128)}), f32[1,8,256]{2,0,1:T(1,128)S(1)}, u32[]{:S(2)}, u32[]{:S(2)}) async-start(f32[1,8,256]{2,0,1:T(1,128)} %copy.55), calls=%async_computation.1 | async-start | bytes 16384 | tf_op jit(solution)/shard_map/all_to_all | solution.py:163
  78.1 3.2 %all-to-all-done.1 = f32[1,8,256]{2,0,1:T(1,128)S(1)} async-done(((f32[1,8,256]{2,0,1:T(1,128)}), f32[1,8,256]{2,0,1:T(1,128)S(1)}, u32[]{:S(2)}, u32[]{:S(2)}) %all-to-all-start.1) | async-done | bytes 8224 | tf_op jit(solution)/shard_map/all_to_all | solution.py:163
  81.3 26.0 %all-reduce.4.cloned.1.call-done = f32[720,45]{0,1:T(8,128)} async-done(((f32[720,45]{0,1:T(8,128)}), f32[720,45]{0,1:T(8,128)}) %all-reduce.4.cloned.1.call-update) | async-done | bytes 129616 | tf_op jit(solution)/shard_map/psum | solution.py:174
  108.4 3.8 %while.21 = (s32[]{:T(128)}, f32[2,1024]{1,0:T(2,128)S(1)}, s32[2,1024]{1,0:T(2,128)S(1)}, s32[2,1024]{1,0:T(2,128)S(1)}, f32[720,45]{1,0:T(8,128)S(1)}, /*index=5*/s32[]{:T(128)}, s32[]{:T(128)}) while((s32[]{:T(128)}, f32[2,1024]{1,0:T(2,128)S(1)}, s32[2,1024]{1,0:T(2,128)S(1)}, s32[2,1024]{1,0:T(2,128)S(1)}, f32[720,45]{1,0:T(8,128)S(1)}, ...), condition=%wide.region_4.5_spmd, body=%wide.region_2.4_spmd.sunk | while | flops 399005696 | bytes 166549 | solution.py:112
  108.5 1.8 %fusion.181 = f32[1024]{0:T(1024)S(1)} fusion(f32[720,45]{1,0:T(8,128)S(1)} %get-tuple-element.253, s32[1024]{0:T(1024)S(1)} %bitcast.169, s32[1024]{0:T(1024)S(1)} %bitcast.170), kind=kOutput, calls=%fused_computation.5.clone.1 | convolution fusion | flops 399005696 | bytes 141888 | tf_op jit(solution)/shard_map/while/body/eval_jaxpr/dot_general | solution.py:104
  112.3 3.1 %while.22 = (s32[]{:T(128)}, f32[45,720]{1,0:T(8,128)S(1)}, s32[2,1024]{1,0:T(2,128)S(1)}, f32[2,1024]{1,0:T(2,128)S(1)}, s32[2,1024]{1,0:T(2,128)S(1)}, /*index=5*/s32[]{:T(128)}, s32[]{:T(128)}) while((s32[]{:T(128)}, f32[45,720]{1,0:T(8,128)S(1)}, s32[2,1024]{1,0:T(2,128)S(1)}, f32[2,1024]{1,0:T(2,128)S(1)}, ...), condition=%wide.region_6.7_spmd.clone, body=%wide.region_5.6_spmd.clone.sunk | while | flops 399025440 | bytes 296159 | solution.py:146
  115.4 3.9 %collective-permute-start.11 = (f32[1,16,720]{2,1,0:T(8,128)S(1)}, f32[1,16,720]{2,1,0:T(8,128)S(1)}, u32[]{:S(2)}, u32[]{:S(2)}) collective-permute-start(f32[1,16,720]{2,1,0:T(8,128)S(1)} %get-tuple-element.117), channel_id=1, source_target_pairs={{0,4},{4,8},{8,12},{12,16},{16,20},{20,24},{24,28},{28,0},{1,5},{5... | collective-permute-start | bytes 138248 | tf_op jit(solution)/shard_map/ppermute | solution.py:43
  120.5 3.2 %collective-permute-done.12 = f32[1,16,720]{2,1,0:T(8,128)S(1)} collective-permute-done((f32[1,16,720]{2,1,0:T(8,128)S(1)}, f32[1,16,720]{2,1,0:T(8,128)S(1)}, u32[]{:S(2)}, u32[]{:S(2)}) %collective-permute-start.12) | collective-permute-done | bytes 46112 | tf_op jit(solution)/shard_map/ppermute | solution.py:46
  123.8 12.7 %fusion.30 = bf16[20,1,45,720]{3,2,0,1:T(8,128)(2,1)S(1)} fusion(bf16[20,16,720]{2,1,0:T(8,128)(2,1)} %bitcast.8, bf16[20,45,720]{2,1,0:T(8,128)(2,1)S(1)} %bitcast.160, bf16[20,16,720]{2,1,0:T(8,128)(2,1)} %bitcast.5, f32[77,720]{1,0:T(8,128)S(1)} %maximum_bitcast_fusion.6, f32[]{:T(128)} %bitcast.41, f32[]{:T(128)} %bitcast.40, f32[]{:T(128)} %bitcast.39, ...), kind=kOutput, calls=%fused_computation.44 | convolution fusion | flops 109497512 | bytes 3735428 | tf_op jit(solution)/shard_map/ij,mljk->mlik/dot_general | solution.py:75
  137.4 11.3 %fusion.23 = f32[20,45,5,144]{3,1,2,0:T(8,128)S(1)} fusion(f32[]{:T(128)} %bitcast.68, f32[]{:T(128)} %bitcast.67, f32[]{:T(128)} %bitcast.66, f32[]{:T(128)} %bitcast.65, f32[]{:T(128)} %bitcast.64, f32[]{:T(128)} %bitcast.63, f32[]{:T(128)} %bitcast.62, f32[]{:T(128)} %bitcast.61, f32[]{:T(128)} %bitcast.60, f32[]{:T(128)} %bitcast.59, f32[]{:T(128)} %bitcast.58, ...), kind=kOutput, calls=%fused_computation.37 | convolution fusion | flops 229439232 | bytes 4176772 | tf_op jit(solution)/shard_map/mlibk,kq->mlibq/dot_general | solution.py:88
  148.6 6.4 %copy.57 = f32[20,45,5,144]{3,2,1,0:T(8,128)} copy(f32[20,45,5,144]{3,1,2,0:T(8,128)S(1)} %fusion.23) | data formatting | bytes 5184000 | tf_op jit(solution)/shard_map/mlibk,kq->mlibq/dot_general | solution.py:88
  155.0 4.9 %reshape.167 = f32[20,1,45,720]{3,2,0,1:T(8,128)S(1)} reshape(f32[20,45,5,144]{3,2,1,0:T(8,128)} %copy.57) | data formatting | bytes 5184000 | tf_op jit(solution)/shard_map/reshape | solution.py:89
  161.6 4.4 %copy.58 = f32[20,1,45,720]{3,1,2,0:T(1,128)} copy(f32[20,1,45,720]{3,2,0,1:T(8,128)S(1)} %convert_add_fusion) | data formatting | bytes 5184000 | tf_op jit(solution)/shard_map/add | solution.py:182
  (80 shorter events, 23.5 us)
Async XLA Ops:
  6.5 28.2 %copy-start = (bf16[20,1,45,720]{3,2,1,0:T(8,128)(2,1)S(1)}, bf16[20,1,45,720]{3,2,1,0:T(8,128)(2,1)}, u32[]{:S(2)}) copy-start(bf16[20,1,45,720]{3,2,1,0:T(8,128)(2,1)} %param.12) | copy-start | bytes 3888004
  6.5 22.8 %copy-start.3 = (f32[1,8,256]{2,1,0:T(8,128)S(1)}, f32[1,8,256]{2,1,0:T(8,128)}, u32[]{:S(2)}) copy-start(f32[1,8,256]{2,1,0:T(8,128)} %param.16) | copy-start | bytes 24580
  8.1 26.6 %collective-permute-start.10 = (bf16[20,1,16,720]{3,2,0,1:T(8,128)(2,1)S(1)}, bf16[20,1,16,720]{3,2,0,1:T(8,128)(2,1)}, u32[]{:S(2)}, u32[]{:S(2)}) collective-permute-start(bf16[20,1,16,720]{3,2,0,1:T(8,128)(2,1)S(1)} %get-tuple-element.114), channel_id=1, source_target_pairs={{4,0},{8,4},{12,8},{16,12},{20,16},{24,20},{28,24},{0,28},{5,1},{9... | collective-permute-start | bytes 1382408 | tf_op jit(solution)/shard_map/ppermute | solution.py:46
  9.8 15.2 %collective-permute-start.2 = (s32[1,1,256]{2,1,0:T(1,128)S(1)}, s32[1,1,256]{2,1,0:T(1,128)S(1)}, u32[]{:S(2)}, u32[]{:S(2)}) collective-permute-start(s32[1,1,256]{2,1,0:T(1,128)S(1)} %get-tuple-element.128), channel_id=1, source_target_pairs={{0,4},{4,0},{8,12},{12,8},{16,20},{20,16},{24,28},{28,24},{1,5},{5... | collective-permute-start | bytes 3080 | tf_op jit(solution)/shard_map/ppermute | solution.py:31
  9.9 16.6 %collective-permute-start.3 = (s32[1,1,256]{2,1,0:T(1,128)S(1)}, s32[1,1,256]{2,1,0:T(1,128)S(1)}, u32[]{:S(2)}, u32[]{:S(2)}) collective-permute-start(s32[1,1,256]{2,1,0:T(1,128)S(1)} %get-tuple-element.127), channel_id=1, source_target_pairs={{0,8},{4,12},{8,0},{12,4},{16,24},{20,28},{24,16},{28,20},{1,9},{5... | collective-permute-start | bytes 3080 | tf_op jit(solution)/shard_map/ppermute | solution.py:31
  12.0 14.7 %collective-permute-start.4 = (s32[1,1,256]{2,1,0:T(1,128)S(1)}, s32[1,1,256]{2,1,0:T(1,128)S(1)}, u32[]{:S(2)}, u32[]{:S(2)}) collective-permute-start(s32[1,1,256]{2,1,0:T(1,128)S(1)} %get-tuple-element.126), channel_id=1, source_target_pairs={{0,12},{4,8},{8,4},{12,0},{16,28},{20,24},{24,20},{28,16},{1,13},{... | collective-permute-start | bytes 3080 | tf_op jit(solution)/shard_map/ppermute | solution.py:31
  12.0 15.8 %collective-permute-start.5 = (s32[1,1,256]{2,1,0:T(1,128)S(1)}, s32[1,1,256]{2,1,0:T(1,128)S(1)}, u32[]{:S(2)}, u32[]{:S(2)}) collective-permute-start(s32[1,1,256]{2,1,0:T(1,128)S(1)} %get-tuple-element.125), channel_id=1, source_target_pairs={{0,16},{4,20},{8,24},{12,28},{16,0},{20,4},{24,8},{28,12},{1,17},{... | collective-permute-start | bytes 3080 | tf_op jit(solution)/shard_map/ppermute | solution.py:31
  14.6 58.4 %all-to-all-start = ((f32[1,8,256]{2,0,1:T(1,128)}), f32[1,8,256]{2,0,1:T(1,128)S(1)}, u32[]{:S(2)}, u32[]{:S(2)}) async-start(f32[1,8,256]{2,0,1:T(1,128)} %compare_select_fusion), calls=%async_computation | async-start | bytes 16384 | tf_op jit(solution)/shard_map/all_to_all | solution.py:164
  18.9 88.5 %all-reduce.4.cloned.1.call-start = ((), (), s32[]{:S(2)}) async-start(), calls=%async_computation.2 | async-start | bytes 294912 | tf_op jit(solution)/shard_map/psum | solution.py:174
  25.0 9.7 %collective-permute-start.9 = (bf16[20,1,16,720]{3,2,0,1:T(8,128)(2,1)S(1)}, bf16[20,1,16,720]{3,2,0,1:T(8,128)(2,1)}, u32[]{:S(2)}, u32[]{:S(2)}) collective-permute-start(bf16[20,1,16,720]{3,2,0,1:T(8,128)(2,1)S(1)} %get-tuple-element.113), channel_id=1, source_target_pairs={{0,4},{4,8},{8,12},{12,16},{16,20},{20,24},{24,28},{28,0},{1,5},{5... | collective-permute-start | bytes 1382408 | tf_op jit(solution)/shard_map/ppermute | solution.py:43
  26.6 3.4 %collective-permute-start.6 = (s32[1,1,256]{2,1,0:T(1,128)S(1)}, s32[1,1,256]{2,1,0:T(1,128)S(1)}, u32[]{:S(2)}, u32[]{:S(2)}) collective-permute-start(s32[1,1,256]{2,1,0:T(1,128)S(1)} %get-tuple-element.124), channel_id=1, source_target_pairs={{0,20},{4,16},{8,28},{12,24},{16,4},{20,0},{24,12},{28,8},{1,21},{... | collective-permute-start | bytes 3080 | tf_op jit(solution)/shard_map/ppermute | solution.py:31
  26.7 7.3 %collective-permute-start.7 = (s32[1,1,256]{2,1,0:T(1,128)S(1)}, s32[1,1,256]{2,1,0:T(1,128)S(1)}, u32[]{:S(2)}, u32[]{:S(2)}) collective-permute-start(s32[1,1,256]{2,1,0:T(1,128)S(1)} %get-tuple-element.130), channel_id=1, source_target_pairs={{0,24},{4,28},{8,16},{12,20},{16,8},{20,12},{24,0},{28,4},{1,25},{... | collective-permute-start | bytes 3080 | tf_op jit(solution)/shard_map/ppermute | solution.py:31
  27.8 6.2 %collective-permute-start.8 = (s32[1,1,256]{2,1,0:T(1,128)S(1)}, s32[1,1,256]{2,1,0:T(1,128)S(1)}, u32[]{:S(2)}, u32[]{:S(2)}) collective-permute-start(s32[1,1,256]{2,1,0:T(1,128)S(1)} %get-tuple-element.123), channel_id=1, source_target_pairs={{0,28},{4,24},{8,20},{12,16},{16,12},{20,8},{24,4},{28,0},{1,29},{... | collective-permute-start | bytes 3080 | tf_op jit(solution)/shard_map/ppermute | solution.py:31
  30.0 93.8 %collective-permute-start = (bf16[20,1,16,720]{3,2,0,1:T(8,128)(2,1)}, bf16[20,1,16,720]{3,2,0,1:T(8,128)(2,1)}, u32[]{:S(2)}, u32[]{:S(2)}) collective-permute-start(bf16[20,1,16,720]{3,2,0,1:T(8,128)(2,1)} %get-tuple-element.115), channel_id=1, source_target_pairs={{0,4},{4,8},{8,12},{12,16},{16,20},{20,24},{24,28},{28,0},{1,5},{5... | collective-permute-start | bytes 1382408 | tf_op jit(solution)/shard_map/ppermute | solution.py:43
  34.0 89.7 %collective-permute-start.1 = (bf16[20,1,16,720]{3,2,0,1:T(8,128)(2,1)S(1)}, bf16[20,1,16,720]{3,2,0,1:T(8,128)(2,1)}, u32[]{:S(2)}, u32[]{:S(2)}) collective-permute-start(bf16[20,1,16,720]{3,2,0,1:T(8,128)(2,1)S(1)} %get-tuple-element.116), channel_id=1, source_target_pairs={{4,0},{8,4},{12,8},{16,12},{20,16},{24,20},{28,24},{0,28},{5,1},{9... | collective-permute-start | bytes 1382408 | tf_op jit(solution)/shard_map/ppermute | solution.py:46
  73.1 8.2 %all-to-all-start.1 = ((f32[1,8,256]{2,0,1:T(1,128)}), f32[1,8,256]{2,0,1:T(1,128)S(1)}, u32[]{:S(2)}, u32[]{:S(2)}) async-start(f32[1,8,256]{2,0,1:T(1,128)} %copy.55), calls=%async_computation.1 | async-start | bytes 16384 | tf_op jit(solution)/shard_map/all_to_all | solution.py:163
  108.4 3.8 %copy-start.2 = (f32[45,720]{1,0:T(8,128)S(1)}, f32[45,720]{1,0:T(8,128)}, u32[]{:S(2)}) copy-start(f32[45,720]{1,0:T(8,128)} %custom-call) | copy-start | bytes 388804
  112.3 11.5 %copy-start.1 = (bf16[20,1,45,720]{3,2,1,0:T(8,128)(2,1)S(1)}, bf16[20,1,45,720]{3,2,1,0:T(8,128)(2,1)}, u32[]{:S(2)}) copy-start(bf16[20,1,45,720]{3,2,1,0:T(8,128)(2,1)} %param.13) | copy-start | bytes 3888004
  115.4 5.1 %collective-permute-start.11 = (f32[1,16,720]{2,1,0:T(8,128)S(1)}, f32[1,16,720]{2,1,0:T(8,128)S(1)}, u32[]{:S(2)}, u32[]{:S(2)}) collective-permute-start(f32[1,16,720]{2,1,0:T(8,128)S(1)} %get-tuple-element.117), channel_id=1, source_target_pairs={{0,4},{4,8},{8,12},{12,16},{16,20},{20,24},{24,28},{28,0},{1,5},{5... | collective-permute-start | bytes 138248 | tf_op jit(solution)/shard_map/ppermute | solution.py:43
  119.3 4.4 %collective-permute-start.12 = (f32[1,16,720]{2,1,0:T(8,128)S(1)}, f32[1,16,720]{2,1,0:T(8,128)S(1)}, u32[]{:S(2)}, u32[]{:S(2)}) collective-permute-start(f32[1,16,720]{2,1,0:T(8,128)S(1)} %get-tuple-element.118), channel_id=1, source_target_pairs={{4,0},{8,4},{12,8},{16,12},{20,16},{24,20},{28,24},{0,28},{5,1},{9... | collective-permute-start | bytes 138248 | tf_op jit(solution)/shard_map/ppermute | solution.py:46
Sparse Core Ops, SparseCore 0:
  73.2 34.1 all-reduce.3
